TPU v7x, 512 devices: a whole 4x8x8 slice. The times are simulated.
512 devices in a mesh: section: 8 (over y), dp: 64 (over x, z, core).
Axes of the slice: x: 4, y: 8, z: 8, core: 2. Of those that a mesh axis runs over, the one named last changes fastest.
Arguments:
- queries: bfloat16 [65536, 3584], P(('section', 'dp')), may hold values from -1 to 1
- passages: bfloat16 [128, 64, 3584], P('dp'), may hold values from -1 to 1
- candidates: int32 [512, 3], P('section'), may hold values from 0 to 63, as said below
- counts: int32 [512], P('section'), may hold values from 1 to 3, 1024 in all
- teacher: float32 [65536, 384], P(('section', 'dp')), may hold values from -20 to 450
- section_weights: bfloat16 [8, 3584, 3584], P('section', 'dp'), may hold values from -0.09375 to 0.09375
- section_inputs: bfloat16 [8, 64, 3584], P('section', None, 'dp'), may hold values from -1.5 to 1.5
- pre_acts: bfloat16 [8, 64, 3584], P('section', None, 'dp'), may hold values from -8 to 8
Outputs:
- query_grads: bfloat16 [65536, 3584], P(('section', 'dp'))
- passage_grads: bfloat16 [128, 64, 3584], P('dp')
- grad_inputs: float32 [8, 64, 3584], P('section', None, 'dp')
- weight_grads: bfloat16 [8, 3584, 3584], P('section', 'dp')
Inputs may be any that keep to these rules, and one draw needn't show every extreme that they name: `candidates`: each row names 3 different passage blocks. A query block uses the first counts[b] entries of its row of candidates.
All inputs are finite; a program needn't handle non-finite values.
Results may differ from a plain program's by a relative error of at most 0.0085.
Values may be sent and summed in bfloat16 or wider, within the bound.
No kernel may reach another device: no remote copies, remote signals or barrier semaphores. Data moves between devices by JAX's collectives and lax.ppermute only.
A program may use at most 64 MiB of HBM per device.

v0:
```python
import jax
import jax.numpy as jnp
from jax import lax
from jax.sharding import PartitionSpec as P

INVERSE_TEMP = 20.0


def passed_along(value, axis, steps):
    count = lax.axis_size(axis)
    initial, last = (max(0, -steps), min(count, count - steps))
    return lax.ppermute(value, axis, [(source, source + steps) for source in range(initial, last)])


def soft_weights(logits, valid):
    masked = jnp.where(valid, logits, -1e30)
    highest = jnp.max(masked, axis=-1, keepdims=True)
    expons = jnp.where(valid, jnp.exp(masked - highest), 0.0)
    return expons / jnp.sum(expons, axis=-1, keepdims=True)


def body(queries, passages, candidates, counts, teacher, section_weights, section_inputs, pre_acts):
    dp_count = lax.axis_size("dp")
    dp_index = lax.axis_index("dp")
    stripe, block_total, width = passages.shape
    row_block_count = stripe * dp_count
    blocks_here = candidates.shape[0] // dp_count
    slot_count = candidates.shape[1]
    requests = blocks_here * slot_count
    all_slots = candidates.reshape(-1)
    outgoing = jnp.take(passages, all_slots, axis=1)
    pulled_rows = lax.all_to_all(outgoing, "dp", split_axis=1, concat_axis=0, tiled=True)
    pulled_rows = pulled_rows.reshape(row_block_count, blocks_here, slot_count, width)
    own_counts = lax.dynamic_slice_in_dim(counts, dp_index * blocks_here, blocks_here)
    slot_valid = jnp.arange(slot_count, dtype=jnp.int32)[None, :] < own_counts[:, None]
    column_valid = jnp.repeat(slot_valid, row_block_count, axis=1)[:, None, :]
    query_row_items = queries.reshape(blocks_here, row_block_count, width)
    logits = (
        jnp.einsum(
            "ixp,wifp->ixfw", query_row_items, pulled_rows, preferred_element_type=jnp.float32
        )
        * INVERSE_TEMP
    )
    logits = logits.reshape(blocks_here, row_block_count, slot_count * row_block_count)
    target_logits = soft_weights(
        teacher.reshape(blocks_here, row_block_count, slot_count * row_block_count), column_valid
    )
    weight_matrices = (soft_weights(logits, column_valid) - target_logits).astype(jnp.bfloat16)
    weight_matrices = weight_matrices.reshape(
        blocks_here, row_block_count, slot_count, row_block_count
    )
    query_sums = (
        jnp.einsum(
            "geal,lgay->gey", weight_matrices, pulled_rows, preferred_element_type=jnp.float32
        )
        * INVERSE_TEMP
    )
    passage_sums = (
        jnp.einsum(
            "fnyw,fnj->wfyj", weight_matrices, query_row_items, preferred_element_type=jnp.float32
        )
        * INVERSE_TEMP
    )
    block_terms = passage_sums.reshape(row_block_count, requests, width).astype(jnp.bfloat16)
    micro_count = section_inputs.shape[1] // dp_count
    col_width = width // dp_count
    micro_cols = jnp.transpose(
        query_sums[0, :micro_count].reshape(micro_count, dp_count, col_width), (1, 0, 2)
    )
    incoming_piece = lax.all_to_all(block_terms, "dp", split_axis=0, concat_axis=1, tiled=True)
    entry = lax.all_to_all(micro_cols, "dp", split_axis=0, concat_axis=1, tiled=True)
    onehot = (all_slots[:, None] == jnp.arange(block_total, dtype=jnp.int32)[None, :]).astype(
        jnp.float32
    )
    dense = jnp.einsum(
        "sjd,jn->snd",
        incoming_piece.astype(jnp.float32),
        onehot,
        precision=lax.Precision.HIGHEST,
        preferred_element_type=jnp.float32,
    )
    passage_out = lax.psum(dense, "section").astype(jnp.bfloat16)
    weight_rows = section_weights[0]
    input_cols = section_inputs[0]
    pre = pre_acts[0].astype(jnp.float32)
    sigma = jax.nn.sigmoid(pre)
    slope = sigma * (1.0 + pre * (1.0 - sigma))
    carry = entry.reshape(dp_count * micro_count, col_width)
    section_count = lax.axis_size("section")
    section_index = lax.axis_index("section")
    grad_cols = jnp.zeros_like(carry)
    grad_weight = jnp.zeros((col_width, width), jnp.float32)
    for section_turn in range(section_count):
        active_flag = section_count - 1 - section_turn
        inner = (carry * slope).astype(jnp.bfloat16)
        piece = lax.all_gather(inner, "dp", axis=1, tiled=True)
        back_sum = jnp.einsum("mj,ij->mi", piece, weight_rows, preferred_element_type=jnp.float32)
        weight_part = jnp.einsum("mi,mj->ij", input_cols, piece, preferred_element_type=jnp.float32)
        back_sum, layer_weight = (back_sum, weight_part)
        updated = carry + back_sum
        is_active = section_index == active_flag
        grad_cols = jnp.where(is_active, updated, grad_cols)
        grad_weight = jnp.where(is_active, layer_weight, grad_weight)
        if section_turn + 1 < section_count:
            carry = passed_along(updated, "section", -1)
    return (
        query_sums.reshape(blocks_here * row_block_count, width).astype(jnp.bfloat16),
        passage_out,
        grad_cols[None],
        grad_weight[None].astype(jnp.bfloat16),
    )


def solution(mesh):
    placed = (
        P(("section", "dp"), None),
        P("dp", None, None),
        P("section", None),
        P("section"),
        P(("section", "dp"), None),
        P("section", "dp", None),
        P("section", None, "dp"),
        P("section", None, "dp"),
    )
    return jax.shard_map(
        body,
        mesh=mesh,
        in_specs=placed,
        out_specs=(
            P(("section", "dp"), None),
            P("dp", None, None),
            P("section", None, "dp"),
            P("section", "dp", None),
        ),
        check_vma=False,
    )
```

profile of v0, /device:TPU:16, one launch (start us, length us, event | category | flops | bytes accessed | tf_op | source)
XLA Modules:
  0.0 732.7 jit_solution(10540011991136659404)
XLA Ops:
  1.8 15.2 %gather_fusion = bf16[192,2,3584]{2,0,1:T(8,128)(2,1)} fusion(bf16[2,64,3584]{2,1,0:T(8,128)(2,1)} %param.9, s32[1024]{0:T(1024)S(1)} %pad_clamp_fusion), kind=kCustom, calls=%fused_computation | custom fusion | bytes 5505792 | tf_op jit(solution)/shard_map/jit(_take)/gather | solution.py:31
  17.0 2.1 select_bitcast_fusion
  19.1 4.4 copy.29
  23.5 14.1 %all-to-all-start = ((bf16[2,192,3584]{2,0,1:T(2,128)(2,1)}), bf16[2,192,3584]{2,0,1:T(2,128)(2,1)}, u32[]{:S(2)}, u32[]{:S(2)}) async-start(bf16[2,192,3584]{2,0,1:T(2,128)(2,1)} %copy.29), calls=%async_computation | async-start | bytes 5505024 | tf_op jit(solution)/shard_map/all_to_all | solution.py:32
  39.5 62.7 %all-to-all-done = bf16[2,192,3584]{2,0,1:T(2,128)(2,1)} async-done(((bf16[2,192,3584]{2,0,1:T(2,128)(2,1)}), bf16[2,192,3584]{2,0,1:T(2,128)(2,1)}, u32[]{:S(2)}, u32[]{:S(2)}) %all-to-all-start) | async-done | bytes 2752544 | tf_op jit(solution)/shard_map/all_to_all | solution.py:32
  102.2 5.2 copy.30
  107.4 6.8 reshape.239
  114.2 2.8 fusion.27
  119.7 6.2 all-to-all-start.2
  126.7 4.2 copy.33
  131.0 4.3 all-to-all-done.2
  135.3 6.4 all-to-all-start.1
  141.8 124.8 %all_gather.24 = bf16[64,3584]{0,1:T(8,128)(2,1)S(1)} all-gather(bf16[64,56]{0,1:T(8,128)(2,1)S(1)} %fusion.38), channel_id=1, replica_groups=mesh['section'=8,'dp'=64] {'dp'}, dimensions={1}, use_global_device_ids=true | all-gather | bytes 465920 | tf_op jit(solution)/shard_map/all_gather | solution.py:96
  266.9 2.8 collective-permute-start
  270.4 2.3 collective-permute-done
  272.7 49.7 %all_gather.25 = bf16[64,3584]{0,1:T(8,128)(2,1)S(1)} all-gather(bf16[64,56]{0,1:T(8,128)(2,1)S(1)} %multiply_convert_fusion.6), channel_id=1, replica_groups=mesh['section'=8,'dp'=64] {'dp'}, dimensions={1}, use_global_device_ids=true | all-gather | bytes 465920 | tf_op jit(solution)/shard_map/all_gather | solution.py:96
  322.7 2.8 collective-permute-start.1
  326.2 2.9 collective-permute-done.1
  329.1 48.2 %all_gather.26 = bf16[64,3584]{0,1:T(8,128)(2,1)S(1)} all-gather(bf16[64,56]{0,1:T(8,128)(2,1)S(1)} %multiply_convert_fusion.5), channel_id=1, replica_groups=mesh['section'=8,'dp'=64] {'dp'}, dimensions={1}, use_global_device_ids=true | all-gather | bytes 465920 | tf_op jit(solution)/shard_map/all_gather | solution.py:96
  377.6 2.2 collective-permute-start.2
  380.5 4.1 collective-permute-done.2
  384.6 50.1 %all_gather.27 = bf16[64,3584]{0,1:T(8,128)(2,1)S(1)} all-gather(bf16[64,56]{0,1:T(8,128)(2,1)S(1)} %multiply_convert_fusion.4), channel_id=1, replica_groups=mesh['section'=8,'dp'=64] {'dp'}, dimensions={1}, use_global_device_ids=true | all-gather | bytes 465920 | tf_op jit(solution)/shard_map/all_gather | solution.py:96
  437.6 4.4 collective-permute-done.3
  442.0 48.2 %all_gather.28 = bf16[64,3584]{0,1:T(8,128)(2,1)S(1)} all-gather(bf16[64,56]{0,1:T(8,128)(2,1)S(1)} %multiply_convert_fusion.3), channel_id=1, replica_groups=mesh['section'=8,'dp'=64] {'dp'}, dimensions={1}, use_global_device_ids=true | all-gather | bytes 465920 | tf_op jit(solution)/shard_map/all_gather | solution.py:96
  493.1 4.4 collective-permute-done.4
  497.5 49.7 %all_gather.29 = bf16[64,3584]{0,1:T(8,128)(2,1)S(1)} all-gather(bf16[64,56]{0,1:T(8,128)(2,1)S(1)} %multiply_convert_fusion.2), channel_id=1, replica_groups=mesh['section'=8,'dp'=64] {'dp'}, dimensions={1}, use_global_device_ids=true | all-gather | bytes 465920 | tf_op jit(solution)/shard_map/all_gather | solution.py:96
  550.0 4.4 collective-permute-done.5
  554.5 48.3 %all_gather.30 = bf16[64,3584]{0,1:T(8,128)(2,1)S(1)} all-gather(bf16[64,56]{0,1:T(8,128)(2,1)S(1)} %multiply_convert_fusion.1), channel_id=1, replica_groups=mesh['section'=8,'dp'=64] {'dp'}, dimensions={1}, use_global_device_ids=true | all-gather | bytes 465920 | tf_op jit(solution)/shard_map/all_gather | solution.py:96
  605.7 4.4 collective-permute-done.6
  610.1 49.7 %all_gather.31 = bf16[64,3584]{0,1:T(8,128)(2,1)S(1)} all-gather(bf16[64,56]{0,1:T(8,128)(2,1)S(1)} %multiply_convert_fusion), channel_id=1, replica_groups=mesh['section'=8,'dp'=64] {'dp'}, dimensions={1}, use_global_device_ids=true | all-gather | bytes 465920 | tf_op jit(solution)/shard_map/all_gather | solution.py:96
  662.1 4.4 copy.34
  667.1 65.4 %all-reduce.1 = bf16[2,64,3584]{2,1,0:T(8,128)(2,1)} all-reduce(f32[2,64,3584]{2,1,0:T(8,128)S(1)} %convolution_bitcast_fusion), channel_id=1, replica_groups=mesh['section'=8,'dp'=64] {'section'}, use_global_device_ids=true, to_apply=%region_4.5 | all-reduce | flops 458752 | bytes 2752512 | tf_op jit(solution)/shard_map/psum | solution.py:82
  (63 shorter events, 23.9 us)
Async XLA Ops:
  0.6 113.6 %copy-start = (bf16[128,3584]{1,0:T(8,128)(2,1)S(1)}, bf16[128,3584]{1,0:T(8,128)(2,1)}, u32[]{:S(2)}) copy-start(bf16[128,3584]{1,0:T(8,128)(2,1)} %param.8) | copy-start | bytes 2752516
  23.5 14.2 %copy-start.5 = (f32[128,384]{1,0:T(8,128)S(1)}, f32[128,384]{1,0:T(8,128)}, u32[]{:S(2)}) copy-start(f32[128,384]{1,0:T(8,128)} %param.12) | copy-start | bytes 589828
  23.5 14.3 %copy-start.6 = (s32[64]{0:T(128)S(1)}, s32[64]{0:T(128)}, u32[]{:S(2)}) copy-start(s32[64]{0:T(128)} %param.11) | copy-start | bytes 772
  23.5 78.7 %all-to-all-start = ((bf16[2,192,3584]{2,0,1:T(2,128)(2,1)}), bf16[2,192,3584]{2,0,1:T(2,128)(2,1)}, u32[]{:S(2)}, u32[]{:S(2)}) async-start(bf16[2,192,3584]{2,0,1:T(2,128)(2,1)} %copy.29), calls=%async_computation | async-start | bytes 5505024 | tf_op jit(solution)/shard_map/all_to_all | solution.py:32
  114.2 3.1 copy-start.1
  119.7 15.6 %all-to-all-start.2 = ((f32[64,1,56]{2,1,0:T(1,128)}), f32[64,1,56]{2,1,0:T(1,128)S(1)}, u32[]{:S(2)}, u32[]{:S(2)}) async-start(f32[64,1,56]{2,1,0:T(1,128)} %bitcast.24), calls=%async_computation.2 | async-start | bytes 65536 | tf_op jit(solution)/shard_map/all_to_all | solution.py:71
  131.0 10.8 %copy-start.4 = (bf16[1,64,56]{1,2,0:T(8,128)(2,1)S(1)}, bf16[1,64,56]{1,2,0:T(8,128)(2,1)}, u32[]{:S(2)}) copy-start(bf16[1,64,56]{1,2,0:T(8,128)(2,1)} %param.15) | copy-start | bytes 21508
  131.0 135.7 %copy-start.2 = (bf16[1,56,3584]{2,1,0:T(8,128)(2,1)S(1)}, bf16[1,56,3584]{2,1,0:T(8,128)(2,1)}, u32[]{:S(2)}) copy-start(bf16[1,56,3584]{2,1,0:T(8,128)(2,1)} %param.13) | copy-start | bytes 1204228
  131.0 138.8 %copy-start.3 = (bf16[1,64,56]{1,2,0:T(8,128)(2,1)S(1)}, bf16[1,64,56]{1,2,0:T(8,128)(2,1)}, u32[]{:S(2)}) copy-start(bf16[1,64,56]{1,2,0:T(8,128)(2,1)} %param.14) | copy-start | bytes 21508
  135.3 526.8 %all-to-all-start.1 = ((bf16[128,3,3584]{2,1,0:T(4,128)(2,1)}), bf16[128,3,3584]{2,1,0:T(4,128)(2,1)}, u32[]{:S(2)}, u32[]{:S(2)}) async-start(bf16[128,3,3584]{2,1,0:T(4,128)(2,1)} %copy.33), calls=%async_computation.1 | async-start | bytes 7340032 | tf_op jit(solution)/shard_map/all_to_all | solution.py:70
  266.9 5.8 collective-permute-start
  322.7 6.4 collective-permute-start.1
  377.6 7.0 collective-permute-start.2
  435.0 7.0 collective-permute-start.3
  490.5 7.0 collective-permute-start.4
  547.4 7.0 collective-permute-start.5
  603.1 7.0 collective-permute-start.6
where the time goes:
time: 742 us; the launch traced here: 733 us
  blocking collectives  534 us (72%)
  waiting for transfers between devices  93.9 us (13%)
  local copies, waits for them, and re-layouts  42.9 us (6%)
  starting transfers between devices  42.2 us (6%)
  matrix products  14.8 us (2%)
    all_gather x8, blocking collectives, body(): piece = lax.all_gather(inner, 'dp', axis=1, tiled=True)  469 us
    psum x1, blocking collectives, body(): passage_out = lax.psum(dense, 'section').astype(jnp.bfloat16)  65.4 us
    all_to_all x1, waiting for transfers between devices, body(): lax.all_to_all(outgoing, 'dp', split_axis=1, concat_axis=0, tiled=True)  62.7 us
    ppermute x7, waiting for transfers between devices, passed_along(): lax.ppermute(value, axis, [(source, source + steps) for source in range(i...  26.8 us
    ppermute x7, starting transfers between devices, passed_along(): lax.ppermute(value, axis, [(source, source + steps) for source in range(i...  15.5 us
    gather x1, local copies, waits for them, and re-layouts, body(): outgoing = jnp.take(passages, all_slots, axis=1)  15.2 us
  transfers between devices with their start and end apart: 10, of which 9 were waited for; matrix products, arithmetic and copies ran while one was open for 2% of the time, Pallas kernels for 0%

commit v1 on v0

--- a/solution.py
+++ b/solution.py
@@ -4,6 +4,10 @@
 from jax.sharding import PartitionSpec as P
 
 INVERSE_TEMP = 20.0
+
+
+def search_the_spots(sheet):
+    return jnp.sum(lax.all_gather(sheet, "section"), 0)
 
 
 def passed_along(value, axis, steps):
@@ -79,7 +83,7 @@
         precision=lax.Precision.HIGHEST,
         preferred_element_type=jnp.float32,
     )
-    passage_out = lax.psum(dense, "section").astype(jnp.bfloat16)
+    passage_out = search_the_spots(dense).astype(jnp.bfloat16)
     weight_rows = section_weights[0]
     input_cols = section_inputs[0]
     pre = pre_acts[0].astype(jnp.float32)

time: 742 us -> 713 us (0.961)
  the two profiles are of different devices: /device:TPU:16 before, /device:TPU:25 now
where the time goes in v1:
time: 713 us; the launch traced here: 704 us
  blocking collectives  490 us (69%)
  waiting for transfers between devices  97.1 us (14%)
  local copies, waits for them, and re-layouts  39.1 us (5%)
  starting transfers between devices  33.9 us (5%)
  matrix products  17.7 us (2%)
  between operations  14.6 us (2%)
  other arithmetic  11.2 us (2%)
    all_gather x8, blocking collectives, body(): piece = lax.all_gather(inner, 'dp', axis=1, tiled=True)  400 us
    all_to_all x1, blocking collectives, body(): lax.all_to_all(block_terms, 'dp', split_axis=0, concat_axis=1, tiled=True)  90.5 us
    all_to_all x1, waiting for transfers between devices, body(): lax.all_to_all(outgoing, 'dp', split_axis=1, concat_axis=0, tiled=True)  63.2 us
    ppermute x7, waiting for transfers between devices, passed_along(): lax.ppermute(value, axis, [(source, source + steps) for source in range(i...  24.7 us
    gather x1, local copies, waits for them, and re-layouts, body(): outgoing = jnp.take(passages, all_slots, axis=1)  15.2 us
    all_to_all x1, starting transfers between devices, body(): lax.all_to_all(outgoing, 'dp', split_axis=1, concat_axis=0, tiled=True)  14.3 us
  transfers between devices with their start and end apart: 10, of which 9 were waited for; matrix products, arithmetic and copies ran while one was open for 2% of the time, Pallas kernels for 0%

profile of v1, /device:TPU:25, one launch (start us, length us, event | category | flops | bytes accessed | tf_op | source)
XLA Modules:
  0.0 704.0 jit_solution(14964517737946096358)
XLA Ops:
  8.3 15.2 %gather_fusion = bf16[192,2,3584]{2,0,1:T(8,128)(2,1)} fusion(bf16[2,64,3584]{2,1,0:T(8,128)(2,1)} %param.9, s32[1024]{0:T(1024)S(1)} %pad_clamp_fusion), kind=kCustom, calls=%fused_computation | custom fusion | bytes 5505792 | tf_op jit(solution)/shard_map/jit(_take)/gather | solution.py:35
  23.6 2.1 select_bitcast_fusion
  25.7 4.4 copy.29
  30.1 14.3 %all-to-all-start = ((bf16[2,192,3584]{2,0,1:T(2,128)(2,1)}), bf16[2,192,3584]{2,0,1:T(2,128)(2,1)}, u32[]{:S(2)}, u32[]{:S(2)}) async-start(bf16[2,192,3584]{2,0,1:T(2,128)(2,1)} %copy.29), calls=%async_computation | async-start | bytes 5505024 | tf_op jit(solution)/shard_map/all_to_all | solution.py:36
  46.2 63.2 %all-to-all-done = bf16[2,192,3584]{2,0,1:T(2,128)(2,1)} async-done(((bf16[2,192,3584]{2,0,1:T(2,128)(2,1)}), bf16[2,192,3584]{2,0,1:T(2,128)(2,1)}, u32[]{:S(2)}, u32[]{:S(2)}) %all-to-all-start) | async-done | bytes 2752544 | tf_op jit(solution)/shard_map/all_to_all | solution.py:36
  109.4 5.2 copy.30
  114.7 6.8 reshape.239
  121.4 2.7 fusion.27
  125.3 2.4 copy.33
  127.7 90.5 %all_to_all.42 = bf16[128,3,3584]{2,1,0:T(4,128)(2,1)S(1)} all-to-all(bf16[128,3,3584]{2,1,0:T(4,128)(2,1)S(1)} %copy.33), channel_id=1, replica_groups=mesh['section'=8,'dp'=64] {'dp'}, dimensions={0} | all-to-all | bytes 5505024 | tf_op jit(solution)/shard_map/all_to_all | solution.py:74
  218.1 2.4 copy.34
  222.4 3.4 fusion.47
  226.6 6.1 all-to-all-start.2
  232.7 9.2 %all-to-all-done.2 = f32[64,1,56]{2,1,0:T(1,128)S(1)} async-done(((f32[64,1,56]{2,1,0:T(1,128)}), f32[64,1,56]{2,1,0:T(1,128)S(1)}, u32[]{:S(2)}, u32[]{:S(2)}) %all-to-all-start.2) | async-done | bytes 14368 | tf_op jit(solution)/shard_map/all_to_all | solution.py:75
  242.1 48.9 %all_gather.32 = bf16[64,3584]{0,1:T(8,128)(2,1)S(1)} all-gather(bf16[64,56]{0,1:T(8,128)(2,1)S(1)} %fusion.38), channel_id=1, replica_groups=mesh['section'=8,'dp'=64] {'dp'}, dimensions={1}, use_global_device_ids=true | all-gather | bytes 465920 | tf_op jit(solution)/shard_map/all_gather | solution.py:100
  291.2 1.9 collective-permute-start
  293.8 4.3 collective-permute-done
  298.2 50.2 %all_gather.33 = bf16[64,3584]{0,1:T(8,128)(2,1)S(1)} all-gather(bf16[64,56]{0,1:T(8,128)(2,1)S(1)} %multiply_convert_fusion.6), channel_id=1, replica_groups=mesh['section'=8,'dp'=64] {'dp'}, dimensions={1}, use_global_device_ids=true | all-gather | bytes 465920 | tf_op jit(solution)/shard_map/all_gather | solution.py:100
  348.7 1.9 collective-permute-start.1
  351.3 4.3 collective-permute-done.1
  355.6 49.5 %all_gather.34 = bf16[64,3584]{0,1:T(8,128)(2,1)S(1)} all-gather(bf16[64,56]{0,1:T(8,128)(2,1)S(1)} %multiply_convert_fusion.5), channel_id=1, replica_groups=mesh['section'=8,'dp'=64] {'dp'}, dimensions={1}, use_global_device_ids=true | all-gather | bytes 465920 | tf_op jit(solution)/shard_map/all_gather | solution.py:100
  408.0 3.2 collective-permute-done.2
  411.3 50.7 %all_gather.35 = bf16[64,3584]{0,1:T(8,128)(2,1)S(1)} all-gather(bf16[64,56]{0,1:T(8,128)(2,1)S(1)} %multiply_convert_fusion.4), channel_id=1, replica_groups=mesh['section'=8,'dp'=64] {'dp'}, dimensions={1}, use_global_device_ids=true | all-gather | bytes 465920 | tf_op jit(solution)/shard_map/all_gather | solution.py:100
  464.8 3.2 collective-permute-done.3
  468.1 49.5 %all_gather.36 = bf16[64,3584]{0,1:T(8,128)(2,1)S(1)} all-gather(bf16[64,56]{0,1:T(8,128)(2,1)S(1)} %multiply_convert_fusion.3), channel_id=1, replica_groups=mesh['section'=8,'dp'=64] {'dp'}, dimensions={1}, use_global_device_ids=true | all-gather | bytes 465920 | tf_op jit(solution)/shard_map/all_gather | solution.py:100
  520.5 3.2 collective-permute-done.4
  523.7 50.8 %all_gather.37 = bf16[64,3584]{0,1:T(8,128)(2,1)S(1)} all-gather(bf16[64,56]{0,1:T(8,128)(2,1)S(1)} %multiply_convert_fusion.2), channel_id=1, replica_groups=mesh['section'=8,'dp'=64] {'dp'}, dimensions={1}, use_global_device_ids=true | all-gather | bytes 465920 | tf_op jit(solution)/shard_map/all_gather | solution.py:100
  577.4 3.2 collective-permute-done.5
  580.7 49.5 %all_gather.38 = bf16[64,3584]{0,1:T(8,128)(2,1)S(1)} all-gather(bf16[64,56]{0,1:T(8,128)(2,1)S(1)} %multiply_convert_fusion.1), channel_id=1, replica_groups=mesh['section'=8,'dp'=64] {'dp'}, dimensions={1}, use_global_device_ids=true | all-gather | bytes 465920 | tf_op jit(solution)/shard_map/all_gather | solution.py:100
  633.1 3.2 collective-permute-done.6
  636.3 50.7 %all_gather.39 = bf16[64,3584]{0,1:T(8,128)(2,1)S(1)} all-gather(bf16[64,56]{0,1:T(8,128)(2,1)S(1)} %multiply_convert_fusion), channel_id=1, replica_groups=mesh['section'=8,'dp'=64] {'dp'}, dimensions={1}, use_global_device_ids=true | all-gather | bytes 465920 | tf_op jit(solution)/shard_map/all_gather | solution.py:100
  689.3 7.7 %reduce_sum.29 = bf16[2,64,3584]{2,1,0:T(8,128)(2,1)} reduce(f32[8,2,64,3584]{3,2,1,0:T(8,128)} %bitcast.160, f32[]{:T(128)} %constant.9.clone.1), dimensions={0}, to_apply=%region_4.5 | reduce | flops 3211264 | bytes 15597572 | tf_op jit(solution)/shard_map/reduce_sum | solution.py:10
  (63 shorter events, 25.5 us)
Async XLA Ops:
  7.2 114.3 %copy-start = (bf16[128,3584]{1,0:T(8,128)(2,1)S(1)}, bf16[128,3584]{1,0:T(8,128)(2,1)}, u32[]{:S(2)}) copy-start(bf16[128,3584]{1,0:T(8,128)(2,1)} %param.8) | copy-start | bytes 2752516
  30.1 14.4 %copy-start.4 = (f32[128,384]{1,0:T(8,128)S(1)}, f32[128,384]{1,0:T(8,128)}, u32[]{:S(2)}) copy-start(f32[128,384]{1,0:T(8,128)} %param.12) | copy-start | bytes 589828
  30.1 14.5 %copy-start.5 = (s32[64]{0:T(128)S(1)}, s32[64]{0:T(128)}, u32[]{:S(2)}) copy-start(s32[64]{0:T(128)} %param.11) | copy-start | bytes 772
  30.1 79.3 %all-to-all-start = ((bf16[2,192,3584]{2,0,1:T(2,128)(2,1)}), bf16[2,192,3584]{2,0,1:T(2,128)(2,1)}, u32[]{:S(2)}, u32[]{:S(2)}) async-start(bf16[2,192,3584]{2,0,1:T(2,128)(2,1)} %copy.29), calls=%async_computation | async-start | bytes 5505024 | tf_op jit(solution)/shard_map/all_to_all | solution.py:36
  44.4 644.9 %all-gather.3.cloned.1.call-start = ((), (), s32[]{:S(2)}) async-start(), calls=%async_computation.3 | async-start | bytes 16515072 | tf_op jit(solution)/shard_map/all_gather | solution.py:10
  222.4 19.6 %copy-start.3 = (bf16[1,64,56]{1,2,0:T(8,128)(2,1)S(1)}, bf16[1,64,56]{1,2,0:T(8,128)(2,1)}, u32[]{:S(2)}) copy-start(bf16[1,64,56]{1,2,0:T(8,128)(2,1)} %param.15) | copy-start | bytes 21508
  222.4 68.5 %copy-start.1 = (bf16[1,56,3584]{2,1,0:T(8,128)(2,1)S(1)}, bf16[1,56,3584]{2,1,0:T(8,128)(2,1)}, u32[]{:S(2)}) copy-start(bf16[1,56,3584]{2,1,0:T(8,128)(2,1)} %param.13) | copy-start | bytes 1204228
  222.4 70.8 %copy-start.2 = (bf16[1,64,56]{1,2,0:T(8,128)(2,1)S(1)}, bf16[1,64,56]{1,2,0:T(8,128)(2,1)}, u32[]{:S(2)}) copy-start(bf16[1,64,56]{1,2,0:T(8,128)(2,1)} %param.14) | copy-start | bytes 21508
  226.6 15.4 %all-to-all-start.2 = ((f32[64,1,56]{2,1,0:T(1,128)}), f32[64,1,56]{2,1,0:T(1,128)S(1)}, u32[]{:S(2)}, u32[]{:S(2)}) async-start(f32[64,1,56]{2,1,0:T(1,128)} %bitcast.25), calls=%async_computation.2 | async-start | bytes 65536 | tf_op jit(solution)/shard_map/all_to_all | solution.py:75
  291.2 6.9 collective-permute-start
  348.7 6.9 collective-permute-start.1
  405.4 5.8 collective-permute-start.2
  462.2 5.8 collective-permute-start.3
  517.9 5.8 collective-permute-start.4
  574.8 5.8 collective-permute-start.5
  630.5 5.8 collective-permute-start.6
Sparse Core Ops, SparseCore 0:
  222.5 152.9 all-gather.2
